TPU v7x, 512 devices: a whole 4x8x8 slice. The times are simulated.
512 devices in a mesh: row: 16 (over y_lo, x), col: 32 (over z, y_hi, core).
Axes of the slice: x: 4, y: 8 (y_hi: 2, y_lo: 4; y = y_hi * 4 + y_lo), z: 8, core: 2. Of those that a mesh axis runs over, the one named last changes fastest.
Arguments:
- precond: float32 [8, 8192, 8192], P(None, 'row', 'col'), may hold values from -6 to 6
- out_factors: bfloat16 [1536, 8192], P('col', 'row'), may hold values from -6 to 6
- in_factors: bfloat16 [1536, 8192], P('row', 'col'), may hold values from -6 to 6
- token_mask: int32 [1536], replicated, may hold values 0 or 1
- seq_ids: int32 [1536], replicated, may hold values from 0 to 3, never falling along the last dimension, each value on 1 to 576 neighbouring positions
- query_ids: int32 [8], replicated, may hold values from 0 to 7, each once
Outputs:
- scores: float32 [8, 4], replicated
Inputs may be any that keep to these rules, and one draw needn't show every extreme that they name: seq_ids never falls along the tokens; each sequence has 1 to 576 tokens. query_ids names each query once.
All inputs are finite; a program needn't handle non-finite values.
Results may differ from a plain program's by a relative error of at most 0.0003.
Values may be sent and summed in bfloat16 or wider, within the bound.
No kernel may reach another device: no remote copies, remote signals or barrier semaphores. Data moves between devices by JAX's collectives and lax.ppermute only.
A program may use at most 64 MiB of HBM per device.

v0:
```python
import math
import jax
import jax.numpy as jnp
from jax import lax
from jax.sharding import PartitionSpec as P

DOUT = 8192
DIN = 8192
SEQ = 4
LEN = 384


def shards(precond, out_factors, in_factors, token_mask, seq_ids, query_ids):
    num_queries = precond.shape[0]
    weight = token_mask.astype(jnp.float32)[:, None] * (
        seq_ids[:, None] == jnp.arange(SEQ, dtype=jnp.int32)[None, :]
    ).astype(jnp.float32)
    out_whole = lax.all_gather(out_factors, "col", axis=0, tiled=True)
    out_wide = out_whole.astype(jnp.float32)
    in_wide = lax.all_gather(in_factors, "row", axis=0, tiled=True).astype(jnp.float32)

    def one_query(query_grad):
        mapped = lax.dot_general(
            in_wide, query_grad, (((1,), (1,)), ((), ())), precision=lax.Precision.HIGHEST
        )
        per_token = jnp.sum(mapped * out_wide, axis=1)
        return jnp.dot(per_token, weight, precision=lax.Precision.HIGHEST)

    total = lax.map(one_query, precond)
    summed = lax.psum(total, ("row", "col"))
    select = (query_ids[:, None] == jnp.arange(num_queries, dtype=jnp.int32)[None, :]).astype(
        jnp.float32
    )
    scale = 1.0 / math.sqrt(DOUT * DIN * LEN)
    return jnp.dot(select, summed, precision=lax.Precision.HIGHEST) * scale


def solution(mesh):
    placed = (P(None, "row", "col"), P("col", "row"), P("row", "col"), P(), P(), P())
    return jax.shard_map(shards, mesh=mesh, in_specs=placed, out_specs=P(), check_vma=False)
```

profile of v0, /device:TPU:1, one launch (start us, length us, event | category | flops | bytes accessed | tf_op | source)
XLA Modules:
  0.0 254.1 jit_solution(18171253237847577728)
XLA Ops:
  6.5 0.0 copy-start
  6.5 0.0 all-gather.2.cloned.1.call-start
  6.5 0.7 all-gather.2.cloned.1.call-update
  7.3 41.4 %all_gather.6 = bf16[1536,256]{1,0:T(8,128)(2,1)S(1)} all-gather(bf16[96,256]{1,0:T(8,128)(2,1)} %param.10), channel_id=1, replica_groups=mesh['row'=16,'col'=32] {'row'}, dimensions={0}, use_global_device_ids=true | all-gather | bytes 835584 | tf_op jit(solution)/shard_map/all_gather | solution.py:20
  48.7 0.0 copy-start.1
  48.7 1.3 convert_element_type.11
  50.0 0.0 copy-done
  50.0 55.2 %all-gather.2.cloned.1.call-done = bf16[1536,512]{1,0:T(8,128)(2,1)} async-done(((bf16[48,512]{1,0:T(8,128)(2,1)}), bf16[1536,512]{1,0:T(8,128)(2,1)}) %all-gather.2.cloned.1.call-update) | async-done | bytes 1572880 | tf_op jit(solution)/shard_map/all_gather | solution.py:18
  105.2 1.8 convert_element_type.12
  107.1 0.0 copy-done.1
  107.1 0.0 copy-start.2
  107.1 42.3 %while.11 = (s32[]{:T(128)}, f32[8,4]{1,0:T(8,128)S(1)}, f32[8,512,256]{2,1,0:T(8,128)}, f32[1536,256]{1,0:T(8,128)}, f32[1536,512]{1,0:T(8,128)S(1)}, /*index=5...) while((s32[]{:T(128)}, f32[8,4]{1,0:T(8,128)S(1)}, f32[8,512,256]{2,1,0:T(8,128)}, ...), condition=%wide.region_2.3_spmd.clone, body=%wide.region_0.2_spmd.clone.sunk | while | flops 2417576448 | bytes 5280401 | solution.py:29
  107.1 4.4 %fusion.27 = f32[1536]{0:T(1024)S(1)} fusion(f32[1536,512]{1,0:T(8,128)S(1)} %get-tuple-element.135, f32[1536,256]{1,0:T(8,128)} %get-tuple-element.134, f32[8,512,256]{2,1,0:T(8,128)} %get-tuple-element.133, s32[]{:T(128)} %get-tuple-element.122), kind=kOutput, calls=%fused_computation.3.clone.1 | convolution fusion | flops 2417490432 | bytes 5249536 | tf_op jit(solution)/shard_map/while/body/eval_jaxpr/dot_general | solution.py:23
  111.5 0.8 fusion.28
  112.4 4.4 %fusion.27 = f32[1536]{0:T(1024)S(1)} fusion(f32[1536,512]{1,0:T(8,128)S(1)} %get-tuple-element.135, f32[1536,256]{1,0:T(8,128)} %get-tuple-element.134, f32[8,512,256]{2,1,0:T(8,128)} %get-tuple-element.133, s32[]{:T(128)} %get-tuple-element.122), kind=kOutput, calls=%fused_computation.3.clone.1 | convolution fusion | flops 2417490432 | bytes 5249536 | tf_op jit(solution)/shard_map/while/body/eval_jaxpr/dot_general | solution.py:23
  116.8 0.8 fusion.28
  117.7 4.4 %fusion.27 = f32[1536]{0:T(1024)S(1)} fusion(f32[1536,512]{1,0:T(8,128)S(1)} %get-tuple-element.135, f32[1536,256]{1,0:T(8,128)} %get-tuple-element.134, f32[8,512,256]{2,1,0:T(8,128)} %get-tuple-element.133, s32[]{:T(128)} %get-tuple-element.122), kind=kOutput, calls=%fused_computation.3.clone.1 | convolution fusion | flops 2417490432 | bytes 5249536 | tf_op jit(solution)/shard_map/while/body/eval_jaxpr/dot_general | solution.py:23
  122.1 0.8 fusion.28
  123.0 4.4 %fusion.27 = f32[1536]{0:T(1024)S(1)} fusion(f32[1536,512]{1,0:T(8,128)S(1)} %get-tuple-element.135, f32[1536,256]{1,0:T(8,128)} %get-tuple-element.134, f32[8,512,256]{2,1,0:T(8,128)} %get-tuple-element.133, s32[]{:T(128)} %get-tuple-element.122), kind=kOutput, calls=%fused_computation.3.clone.1 | convolution fusion | flops 2417490432 | bytes 5249536 | tf_op jit(solution)/shard_map/while/body/eval_jaxpr/dot_general | solution.py:23
  127.4 0.8 fusion.28
  128.3 4.4 %fusion.27 = f32[1536]{0:T(1024)S(1)} fusion(f32[1536,512]{1,0:T(8,128)S(1)} %get-tuple-element.135, f32[1536,256]{1,0:T(8,128)} %get-tuple-element.134, f32[8,512,256]{2,1,0:T(8,128)} %get-tuple-element.133, s32[]{:T(128)} %get-tuple-element.122), kind=kOutput, calls=%fused_computation.3.clone.1 | convolution fusion | flops 2417490432 | bytes 5249536 | tf_op jit(solution)/shard_map/while/body/eval_jaxpr/dot_general | solution.py:23
  132.7 0.8 fusion.28
  133.6 4.4 %fusion.27 = f32[1536]{0:T(1024)S(1)} fusion(f32[1536,512]{1,0:T(8,128)S(1)} %get-tuple-element.135, f32[1536,256]{1,0:T(8,128)} %get-tuple-element.134, f32[8,512,256]{2,1,0:T(8,128)} %get-tuple-element.133, s32[]{:T(128)} %get-tuple-element.122), kind=kOutput, calls=%fused_computation.3.clone.1 | convolution fusion | flops 2417490432 | bytes 5249536 | tf_op jit(solution)/shard_map/while/body/eval_jaxpr/dot_general | solution.py:23
  138.0 0.8 fusion.28
  138.8 4.4 %fusion.27 = f32[1536]{0:T(1024)S(1)} fusion(f32[1536,512]{1,0:T(8,128)S(1)} %get-tuple-element.135, f32[1536,256]{1,0:T(8,128)} %get-tuple-element.134, f32[8,512,256]{2,1,0:T(8,128)} %get-tuple-element.133, s32[]{:T(128)} %get-tuple-element.122), kind=kOutput, calls=%fused_computation.3.clone.1 | convolution fusion | flops 2417490432 | bytes 5249536 | tf_op jit(solution)/shard_map/while/body/eval_jaxpr/dot_general | solution.py:23
  143.3 0.8 fusion.28
  144.1 4.4 %fusion.27 = f32[1536]{0:T(1024)S(1)} fusion(f32[1536,512]{1,0:T(8,128)S(1)} %get-tuple-element.135, f32[1536,256]{1,0:T(8,128)} %get-tuple-element.134, f32[8,512,256]{2,1,0:T(8,128)} %get-tuple-element.133, s32[]{:T(128)} %get-tuple-element.122), kind=kOutput, calls=%fused_computation.3.clone.1 | convolution fusion | flops 2417490432 | bytes 5249536 | tf_op jit(solution)/shard_map/while/body/eval_jaxpr/dot_general | solution.py:23
  148.5 0.8 fusion.28
  149.4 97.1 %psum.7 = f32[8,4]{1,0:T(8,128)S(1)} all-reduce(f32[8,4]{1,0:T(8,128)S(1)} %get-tuple-element.37), channel_id=1, replica_groups=mesh['row'=16,'col'=32] {'row','col'}, use_global_device_ids=true, to_apply=%region_3.4 | all-reduce | flops 32 | bytes 256 | tf_op jit(solution)/shard_map/psum | solution.py:30
  246.5 0.0 copy-done.2
  246.5 0.8 convolution_multiply_fusion
  (18 shorter events, 0.3 us)
Async XLA Ops:
  6.5 43.5 %copy-start = (s32[1536]{0:T(1024)S(1)}, s32[1536]{0:T(1024)}, u32[]{:S(2)}) copy-start(s32[1536]{0:T(1024)} %param.11) | copy-start | bytes 18436
  6.5 98.7 %all-gather.2.cloned.1.call-start = ((), (), s32[]{:S(2)}) async-start(), calls=%async_computation | async-start | bytes 1622016 | tf_op jit(solution)/shard_map/all_gather | solution.py:18
  48.7 58.4 %copy-start.1 = (s32[1536]{0:T(1024)S(1)}, s32[1536]{0:T(1024)}, u32[]{:S(2)}) copy-start(s32[1536]{0:T(1024)} %param.12) | copy-start | bytes 18436
  107.1 139.4 %copy-start.2 = (s32[8]{0:T(128)S(1)}, s32[8]{0:T(128)}, u32[]{:S(2)}) copy-start(s32[8]{0:T(128)} %param.13) | copy-start | bytes 100
Sparse Core Ops, SparseCore 0:
  10.7 94.5 all-gather.1
where the time goes:
time: 255 us; the launch traced here: 254 us
  blocking collectives  139 us (55%)
  waiting for transfers between devices  56 us (22%)
  matrix products  42.5 us (17%)
  between operations  13.4 us (5%)
  other arithmetic  3.12 us (1%)
    psum x1, blocking collectives, shards(): summed = lax.psum(total, ('row', 'col'))  97.1 us
    all_gather x1, waiting for transfers between devices, shards(): out_whole = lax.all_gather(out_factors, 'col', axis=0, tiled=True)  55.2 us
    all_gather x1, blocking collectives, shards(): lax.all_gather(in_factors, 'row', axis=0, tiled=True).astype(jnp.float32)  41.4 us
    dot_general x8, matrix products, one_query(): lax.dot_general(in_wide, query_grad, (((1,), (1,)), ((), ())), precision=...  35.2 us
    dot_general x8, matrix products, one_query(): return jnp.dot(per_token, weight, precision=lax.Precision.HIGHEST)  6.58 us
  transfers between devices with their start and end apart: 1, of which 1 were waited for; matrix products, arithmetic and copies ran while one was open for 1% of the time, Pallas kernels for 0%

commit v1 on v0

--- a/solution.py
+++ b/solution.py
@@ -15,7 +15,9 @@
     weight = token_mask.astype(jnp.float32)[:, None] * (
         seq_ids[:, None] == jnp.arange(SEQ, dtype=jnp.int32)[None, :]
     ).astype(jnp.float32)
-    out_whole = lax.all_gather(out_factors, "col", axis=0, tiled=True)
+    out_whole = jnp.concatenate(
+        lax.all_to_all(jnp.stack([out_factors] * lax.axis_size("col")), "col", 0, 0), axis=0
+    )
     out_wide = out_whole.astype(jnp.float32)
     in_wide = lax.all_gather(in_factors, "row", axis=0, tiled=True).astype(jnp.float32)
 

time: 255 us -> 240 us (0.941)
  waiting for transfers between devices: 56 us -> 0.01 us
  blocking collectives: 139 us -> 174 us
  starting transfers between devices: 0.01 us -> 17.4 us
  between operations: 13.4 us -> 0.06 us
    all_gather x1 -> x0, waiting for transfers between devices: 55.2 us -> none  [shards(): out_whole = lax.all_gather(out_factors, 'col', axis=0, tiled=True)]
    all_gather x1, blocking collectives: 41.4 us -> 67.8 us  [shards(): lax.all_gather(in_factors, 'row', axis=0, tiled=True).astype(jnp.float32)]
    all_to_all x0 -> x1, starting transfers between devices: none -> 17.4 us  [shards(): lax.all_to_all(jnp.stack([out_factors] * lax.axis_size('col')), 'col', 0, 0)]
    psum x1, blocking collectives: 97.1 us -> 106 us  [shards(): summed = lax.psum(total, ('row', 'col'))]
  transfers between devices with their start and end apart: 1 -> 1, of which waited for: 1 -> 0; matrix products, arithmetic and copies ran while one was open for 1% -> 1% of each run, Pallas kernels for 0% -> 0%
where the time goes in v1:
time: 240 us
  blocking collectives  174 us (72%)
  matrix products  42.5 us (18%)
  starting transfers between devices  17.4 us (7%)
  other arithmetic  3.12 us (1%)
  local copies, waits for them, and re-layouts  2.48 us (1%)
    psum x1, blocking collectives, shards(): summed = lax.psum(total, ('row', 'col'))  106 us
    all_gather x1, blocking collectives, shards(): lax.all_gather(in_factors, 'row', axis=0, tiled=True).astype(jnp.float32)  67.8 us
    dot_general x8, matrix products, one_query(): lax.dot_general(in_wide, query_grad, (((1,), (1,)), ((), ())), precision=...  35.2 us
    all_to_all x1, starting transfers between devices, shards(): lax.all_to_all(jnp.stack([out_factors] * lax.axis_size('col')), 'col', 0, 0)  17.4 us
    dot_general x8, matrix products, one_query(): return jnp.dot(per_token, weight, precision=lax.Precision.HIGHEST)  6.58 us
  transfers between devices with their start and end apart: 1, of which 0 were waited for; matrix products, arithmetic and copies ran while one was open for 1% of the time, Pallas kernels for 0%

profile of v1, /device:TPU:1, one launch (start us, length us, event | category | flops | bytes accessed | tf_op | source)
XLA Modules:
  0.0 239.8 jit_solution(13347727869896359610)
XLA Ops:
  0.0 0.0 copy-start
  0.0 2.1 stack.2
  2.1 0.0 copy-start.1
  2.1 17.4 %all-to-all-start = ((bf16[32,48,512]{2,1,0:T(8,128)(2,1)}), bf16[32,48,512]{2,1,0:T(8,128)(2,1)}, u32[]{:S(2)}, u32[]{:S(2)}) async-start(bf16[32,48,512]{2,1,0:T(8,128)(2,1)} %stack.2), calls=%async_computation | async-start | bytes 3145728 | tf_op jit(solution)/shard_map/all_to_all | solution.py:19
  19.5 0.0 copy-done
  19.6 67.8 %all_gather.3 = bf16[1536,256]{1,0:T(8,128)(2,1)S(1)} all-gather(bf16[96,256]{1,0:T(8,128)(2,1)S(1)} %copy-done), channel_id=1, replica_groups=mesh['row'=16,'col'=32] {'row'}, dimensions={0}, use_global_device_ids=true | all-gather | bytes 835584 | tf_op jit(solution)/shard_map/all_gather | solution.py:22
  87.4 0.0 copy-start.2
  87.4 1.3 convert_element_type.14
  88.7 0.0 copy-done.1
  88.7 0.0 all-to-all-done
  88.7 1.8 bitcast_convert_fusion
  90.5 0.0 copy-done.2
  90.5 0.0 copy-start.3
  90.5 42.3 %while.11 = (s32[]{:T(128)}, f32[8,4]{1,0:T(8,128)S(1)}, f32[8,512,256]{2,1,0:T(8,128)}, f32[1536,256]{1,0:T(8,128)}, f32[1536,512]{1,0:T(8,128)S(1)}, /*index=5...) while((s32[]{:T(128)}, f32[8,4]{1,0:T(8,128)S(1)}, f32[8,512,256]{2,1,0:T(8,128)}, ...), condition=%wide.region_2.3_spmd.clone, body=%wide.region_0.2_spmd.clone.sunk | while | flops 2417576448 | bytes 5280401 | solution.py:31
  90.5 4.4 %fusion.27 = f32[1536]{0:T(1024)S(1)} fusion(f32[1536,512]{1,0:T(8,128)S(1)} %get-tuple-element.135, f32[1536,256]{1,0:T(8,128)} %get-tuple-element.134, f32[8,512,256]{2,1,0:T(8,128)} %get-tuple-element.133, s32[]{:T(128)} %get-tuple-element.122), kind=kOutput, calls=%fused_computation.3.clone.1 | convolution fusion | flops 2417490432 | bytes 5249536 | tf_op jit(solution)/shard_map/while/body/eval_jaxpr/dot_general | solution.py:25
  95.0 0.8 fusion.28
  95.8 4.4 %fusion.27 = f32[1536]{0:T(1024)S(1)} fusion(f32[1536,512]{1,0:T(8,128)S(1)} %get-tuple-element.135, f32[1536,256]{1,0:T(8,128)} %get-tuple-element.134, f32[8,512,256]{2,1,0:T(8,128)} %get-tuple-element.133, s32[]{:T(128)} %get-tuple-element.122), kind=kOutput, calls=%fused_computation.3.clone.1 | convolution fusion | flops 2417490432 | bytes 5249536 | tf_op jit(solution)/shard_map/while/body/eval_jaxpr/dot_general | solution.py:25
  100.2 0.8 fusion.28
  101.1 4.4 %fusion.27 = f32[1536]{0:T(1024)S(1)} fusion(f32[1536,512]{1,0:T(8,128)S(1)} %get-tuple-element.135, f32[1536,256]{1,0:T(8,128)} %get-tuple-element.134, f32[8,512,256]{2,1,0:T(8,128)} %get-tuple-element.133, s32[]{:T(128)} %get-tuple-element.122), kind=kOutput, calls=%fused_computation.3.clone.1 | convolution fusion | flops 2417490432 | bytes 5249536 | tf_op jit(solution)/shard_map/while/body/eval_jaxpr/dot_general | solution.py:25
  105.5 0.8 fusion.28
  106.4 4.4 %fusion.27 = f32[1536]{0:T(1024)S(1)} fusion(f32[1536,512]{1,0:T(8,128)S(1)} %get-tuple-element.135, f32[1536,256]{1,0:T(8,128)} %get-tuple-element.134, f32[8,512,256]{2,1,0:T(8,128)} %get-tuple-element.133, s32[]{:T(128)} %get-tuple-element.122), kind=kOutput, calls=%fused_computation.3.clone.1 | convolution fusion | flops 2417490432 | bytes 5249536 | tf_op jit(solution)/shard_map/while/body/eval_jaxpr/dot_general | solution.py:25
  110.8 0.8 fusion.28
  111.7 4.4 %fusion.27 = f32[1536]{0:T(1024)S(1)} fusion(f32[1536,512]{1,0:T(8,128)S(1)} %get-tuple-element.135, f32[1536,256]{1,0:T(8,128)} %get-tuple-element.134, f32[8,512,256]{2,1,0:T(8,128)} %get-tuple-element.133, s32[]{:T(128)} %get-tuple-element.122), kind=kOutput, calls=%fused_computation.3.clone.1 | convolution fusion | flops 2417490432 | bytes 5249536 | tf_op jit(solution)/shard_map/while/body/eval_jaxpr/dot_general | solution.py:25
  116.1 0.8 fusion.28
  117.0 4.4 %fusion.27 = f32[1536]{0:T(1024)S(1)} fusion(f32[1536,512]{1,0:T(8,128)S(1)} %get-tuple-element.135, f32[1536,256]{1,0:T(8,128)} %get-tuple-element.134, f32[8,512,256]{2,1,0:T(8,128)} %get-tuple-element.133, s32[]{:T(128)} %get-tuple-element.122), kind=kOutput, calls=%fused_computation.3.clone.1 | convolution fusion | flops 2417490432 | bytes 5249536 | tf_op jit(solution)/shard_map/while/body/eval_jaxpr/dot_general | solution.py:25
  121.4 0.8 fusion.28
  122.3 4.4 %fusion.27 = f32[1536]{0:T(1024)S(1)} fusion(f32[1536,512]{1,0:T(8,128)S(1)} %get-tuple-element.135, f32[1536,256]{1,0:T(8,128)} %get-tuple-element.134, f32[8,512,256]{2,1,0:T(8,128)} %get-tuple-element.133, s32[]{:T(128)} %get-tuple-element.122), kind=kOutput, calls=%fused_computation.3.clone.1 | convolution fusion | flops 2417490432 | bytes 5249536 | tf_op jit(solution)/shard_map/while/body/eval_jaxpr/dot_general | solution.py:25
  126.7 0.8 fusion.28
  127.6 4.4 %fusion.27 = f32[1536]{0:T(1024)S(1)} fusion(f32[1536,512]{1,0:T(8,128)S(1)} %get-tuple-element.135, f32[1536,256]{1,0:T(8,128)} %get-tuple-element.134, f32[8,512,256]{2,1,0:T(8,128)} %get-tuple-element.133, s32[]{:T(128)} %get-tuple-element.122), kind=kOutput, calls=%fused_computation.3.clone.1 | convolution fusion | flops 2417490432 | bytes 5249536 | tf_op jit(solution)/shard_map/while/body/eval_jaxpr/dot_general | solution.py:25
  132.0 0.8 fusion.28
  132.8 106.2 %psum.7 = f32[8,4]{1,0:T(8,128)S(1)} all-reduce(f32[8,4]{1,0:T(8,128)S(1)} %get-tuple-element.37), channel_id=1, replica_groups=mesh['row'=16,'col'=32] {'row','col'}, use_global_device_ids=true, to_apply=%region_3.4 | all-reduce | flops 32 | bytes 256 | tf_op jit(solution)/shard_map/psum | solution.py:32
  239.0 0.0 copy-done.3
  239.1 0.8 convolution_multiply_fusion
  (18 shorter events, 0.3 us)
Async XLA Ops:
  0.0 19.6 %copy-start = (bf16[96,256]{1,0:T(8,128)(2,1)S(1)}, bf16[96,256]{1,0:T(8,128)(2,1)}, u32[]{:S(2)}) copy-start(bf16[96,256]{1,0:T(8,128)(2,1)} %param.10) | copy-start | bytes 147460
  2.1 86.5 %copy-start.1 = (s32[1536]{0:T(1024)S(1)}, s32[1536]{0:T(1024)}, u32[]{:S(2)}) copy-start(s32[1536]{0:T(1024)} %param.11) | copy-start | bytes 18436
  2.1 86.5 %all-to-all-start = ((bf16[32,48,512]{2,1,0:T(8,128)(2,1)}), bf16[32,48,512]{2,1,0:T(8,128)(2,1)}, u32[]{:S(2)}, u32[]{:S(2)}) async-start(bf16[32,48,512]{2,1,0:T(8,128)(2,1)} %stack.2), calls=%async_computation | async-start | bytes 3145728 | tf_op jit(solution)/shard_map/all_to_all | solution.py:19
  87.4 3.1 %copy-start.2 = (s32[1536]{0:T(1024)S(1)}, s32[1536]{0:T(1024)}, u32[]{:S(2)}) copy-start(s32[1536]{0:T(1024)} %param.12) | copy-start | bytes 18436
  90.5 148.5 %copy-start.3 = (s32[8]{0:T(128)S(1)}, s32[8]{0:T(128)}, u32[]{:S(2)}) copy-start(s32[8]{0:T(128)} %param.13) | copy-start | bytes 100
